TPU v7x, 32 devices: a whole 2x2x4 slice. The times are simulated.
32 devices in a mesh: req: 4 (over y, x), cand: 8 (over z, core).
Axes of the slice: x: 2, y: 2, z: 4, core: 2. Of those that a mesh axis runs over, the one named last changes fastest.
Arguments:
- table: bfloat16 [32768, 256], P('req'), may hold values from -6 to 6
- history_shard: int32 [4, 1024, 1], P('req', 'cand'), may hold values from 0 to 3; in each aligned block of 128 rows (0 to 127, 128 to 255, ..., all dimensions but the last counted through in order) at most 128 rows name the same one
- history_row: int32 [4, 1024], P('req', 'cand'), may hold values from 0 to 8191
- candidate_shard: int32 [4, 2048, 1], P('req', 'cand'), may hold values from 0 to 3; in each aligned block of 256 rows (0 to 255, 256 to 511, ..., all dimensions but the last counted through in order) at most 192 rows name the same one
- candidate_row: int32 [4, 2048], P('req', 'cand'), may hold values from 0 to 8191
- history_length: int32 [4], P('req'), may hold values from 128 to 1024, as said below
- w_query: bfloat16 [256, 256], replicated, may hold values from -0.375 to 0.375
- w_key: bfloat16 [256, 256], replicated, may hold values from -0.375 to 0.375
- w_value: bfloat16 [256, 256], replicated, may hold values from -0.375 to 0.375
- tower_in: bfloat16 [512, 1024], replicated, may hold values from -0.25 to 0.25
- tower_out: bfloat16 [1024], replicated, may hold values from -0.1875 to 0.1875
Outputs:
- logits: float32 [4, 2048], P('req', 'cand')
Inputs may be any that keep to these rules, and one draw needn't show every extreme that they name: `history_shard`: among the 128 events of one request that one device holds, at most 128 name the same table shard, a bound that some block reaches. `candidate_shard`: among the 256 candidates of one request that one device holds, at most 192 name the same table shard, a bound that some block reaches. `history_length`: some request has all 1024 events live.
All inputs are finite; a program needn't handle non-finite values.
Results may differ from a plain program's by a relative error of at most 0.004.
Values may be sent and summed in bfloat16 or wider, within the bound.
No kernel may reach another device: no remote copies, remote signals or barrier semaphores. Data moves between devices by JAX's collectives and lax.ppermute only.
A program may use at most 64 MiB of HBM per device.

v0:
```python
import math
import jax
import jax.numpy as jnp
from jax import lax
from jax.sharding import PartitionSpec as P

HEADS = 4


def slot_index(shard_ids, n_dest, slot_count, first_slot):
    onehot = (shard_ids[:, None] == jnp.arange(n_dest, dtype=jnp.int32)[None, :]).astype(jnp.int32)
    before = jnp.cumsum(onehot, axis=0) - onehot
    rank = jnp.sum(before * onehot, axis=1)
    return shard_ids * slot_count + first_slot + rank


def body(
    table,
    history_shard,
    history_row,
    candidate_shard,
    candidate_row,
    history_length,
    w_query,
    w_key,
    w_value,
    tower_in,
    tower_out,
):
    n_dest = lax.axis_size("req")
    d_model = table.shape[1]
    hist_shards = history_shard[0, :, 0]
    cand_shards = candidate_shard[0, :, 0]
    hist_dev = hist_shards.shape[0]
    cand_dev = cand_shards.shape[0]
    hist_cap = 4 * hist_dev // n_dest
    cand_cap = 3 * cand_dev // n_dest
    slot_count = hist_cap + cand_cap
    hist_slot = slot_index(hist_shards, n_dest, slot_count, 0)
    cand_slot = slot_index(cand_shards, n_dest, slot_count, hist_cap)
    wanted = jnp.zeros((n_dest * slot_count,), jnp.int32)
    wanted = wanted.at[hist_slot].set(history_row[0]).at[cand_slot].set(candidate_row[0])
    wanted = wanted.reshape(n_dest, slot_count)
    fetched = jnp.take(
        table, lax.all_to_all(wanted, "req", split_axis=0, concat_axis=0, tiled=True), axis=0
    )
    replies = lax.all_to_all(fetched, "req", split_axis=0, concat_axis=0, tiled=True)
    flat_rows = replies.reshape(n_dest * slot_count, d_model)
    hist_emb = jnp.take(flat_rows, hist_slot, axis=0)
    cand_emb = jnp.take(flat_rows, cand_slot, axis=0)
    head_size = d_model // HEADS
    scale_factor = 1.0 / math.sqrt(head_size)
    length = history_length[0]
    w_pair = jnp.concatenate([w_key, w_value], axis=1)
    query_row_matrix = jnp.dot(cand_emb, w_query, preferred_element_type=jnp.float32).astype(
        jnp.bfloat16
    )
    query_row_matrix = query_row_matrix.reshape(cand_dev, HEADS, head_size)
    pair_local = jnp.dot(hist_emb, w_pair, preferred_element_type=jnp.float32).astype(jnp.bfloat16)
    pair_rows = lax.all_gather(pair_local, "cand", axis=0, tiled=True)
    count = pair_rows.shape[0]
    key_portion_slice = pair_rows[:, :d_model].reshape(count, HEADS, head_size)
    value_portion_slice = pair_rows[:, d_model:].reshape(count, HEADS, head_size)
    score_matrix = (
        jnp.einsum(
            "zun,aun->zua", query_row_matrix, key_portion_slice, preferred_element_type=jnp.float32
        )
        * scale_factor
    )
    live_mask = jnp.arange(count, dtype=jnp.int32) < length
    gate_weights = jnp.where(
        live_mask[None, None, :], jax.nn.sigmoid(score_matrix), jnp.float32(0.0)
    ).astype(jnp.bfloat16)
    weighted_sum = jnp.einsum(
        "bgo,ogl->bgl", gate_weights, value_portion_slice, preferred_element_type=jnp.float32
    )
    attended = (
        (weighted_sum / jnp.sqrt(length.astype(jnp.float32)))
        .reshape(cand_dev, d_model)
        .astype(jnp.bfloat16)
    )
    pre_act = jnp.dot(cand_emb, tower_in[:d_model], preferred_element_type=jnp.float32) + jnp.dot(
        attended, tower_in[d_model:], preferred_element_type=jnp.float32
    )
    hidden = jax.nn.silu(pre_act).astype(jnp.bfloat16)
    return jnp.dot(hidden, tower_out, preferred_element_type=jnp.float32)[None, :]


def solution(mesh):
    placed = (
        P("req", None),
        P("req", "cand", None),
        P("req", "cand"),
        P("req", "cand", None),
        P("req", "cand"),
        P("req"),
        P(),
        P(),
        P(),
        P(),
        P(),
    )
    return jax.shard_map(
        body, mesh=mesh, in_specs=placed, out_specs=P("req", "cand"), check_vma=False
    )
```

profile of v0, /device:TPU:0, one launch (start us, length us, event | category | flops | bytes accessed | tf_op | source)
XLA Modules:
  0.0 80.8 jit_solution(6493712422928214452)
XLA Ops:
  6.5 0.0 copy-start
  6.5 0.7 compare_convert_fusion
  7.3 1.2 %reduce-window.6 = s32[4,2,128]{2,1,0:T(2,128)S(1)} reduce-window(s32[4,2,128]{2,1,0:T(2,128)S(1)} %compare_convert_fusion, s32[]{:T(128)} %constant.41.clone.1), window={size=1x1x128 pad=0_0x0_0x127_0}, to_apply=%region_0.0 | reduce-window | flops 130048 | bytes 8196 | tf_op jit(solution)/shard_map/reduce-window
  8.5 0.1 slice.30
  8.5 0.1 copy.19
  8.7 0.1 copy.20
  8.8 0.1 add_bitcast_fusion
  8.9 0.7 fusion.24
  9.6 0.7 compare_select_fusion.2
  10.2 0.7 fusion.18
  11.0 0.2 reduce_window_sum.28
  11.2 0.8 %select_reduce_fusion = s32[128]{0:T(128)S(1)} fusion(s32[128,4]{1,0:T(8,128)S(1)} %reduce_window_sum.28, s32[128]{0:T(128)} %bitcast.86), kind=kLoop, calls=%fused_computation.25 | loop fusion | flops 2432 | bytes 3072 | tf_op jit(solution)/shard_map/reduce_sum | solution.py:13
  12.0 0.7 fusion.27
  12.7 1.1 %scatter_custom_fusion = s32[1280]{0:T(1024)S(1)} fusion(s32[128]{0:T(128)S(1)} %fusion.27, s32[128]{0:T(128)} %bitcast.88, s32[]{:T(128)} %constant.41.clone.1), kind=kCustom, calls=%fused_computation.44 | custom fusion | bytes 5632 | tf_op jit(solution)/shard_map/scatter | solution.py:42
  13.8 1.6 %scatter_fusion = s32[1280]{0:T(1024)S(1)} fusion(s32[1280]{0:T(1024)S(1)} %scatter_custom_fusion, s32[256]{0:T(256)S(1)} %bitcast.81, s32[256]{0:T(256)} %bitcast.87), kind=kCustom, calls=%fused_computation.4 | custom fusion | bytes 4096 | tf_op jit(solution)/shard_map/scatter | solution.py:42
  15.4 0.1 all_to_all.13
  15.4 9.6 %all_to_all.20 = s32[4,1,320]{2,1,0:T(1,128)S(1)} all-to-all(s32[4,1,320]{2,1,0:T(1,128)S(1)} %all_to_all.13), channel_id=1, replica_groups=mesh['req'=4,'cand'=8] {'req'}, dimensions={0} | all-to-all | bytes 10240 | tf_op jit(solution)/shard_map/all_to_all | solution.py:45
  25.1 0.1 reshape.156
  25.2 0.0 copy-start.3
  25.2 0.0 copy-start.5
  25.2 0.0 copy-start.6
  25.2 0.0 copy-start.4
  25.2 0.0 copy-start.2
  25.3 5.9 %gather_fusion = bf16[1280,256]{1,0:T(8,128)(2,1)S(1)} fusion(bf16[8192,256]{1,0:T(8,128)(2,1)} %param.11, s32[2048]{0:T(1024)S(1)} %pad_clamp_fusion), kind=kCustom, calls=%fused_computation | custom fusion | bytes 1315840 | tf_op jit(solution)/shard_map/jit(_take)/gather | solution.py:44
  31.2 0.0 copy-start.1
  31.2 1.1 %broadcast_select_fusion = bf16[4,320,256]{2,1,0:T(8,128)(2,1)} fusion(bf16[4,320,256]{2,1,0:T(8,128)(2,1)S(1)} %bitcast.74, pred[4,320]{1,0:T(4,128)(4,1)S(1)} %compare_and_fusion), kind=kLoop, calls=%fused_computation.15 | loop fusion | flops 327680 | bytes 1312000 | tf_op jit(solution)/shard_map/jit(_take)/select_n | solution.py:44
  32.3 3.5 %all-to-all-start.1 = ((bf16[4,320,256]{2,1,0:T(8,128)(2,1)}), bf16[4,320,256]{2,1,0:T(8,128)(2,1)S(1)}, u32[]{:S(2)}, u32[]{:S(2)}) async-start(bf16[4,320,256]{2,1,0:T(8,128)(2,1)} %broadcast_select_fusion), calls=%async_computation.1 | async-start | bytes 1310720 | tf_op jit(solution)/shard_map/all_to_all | solution.py:47
  35.8 0.0 all-gather.2.cloned.1.call-start
  35.9 0.0 copy-done.3
  35.9 8.1 %all-to-all-done.1 = bf16[4,320,256]{2,1,0:T(8,128)(2,1)S(1)} async-done(((bf16[4,320,256]{2,1,0:T(8,128)(2,1)}), bf16[4,320,256]{2,1,0:T(8,128)(2,1)S(1)}, u32[]{:S(2)}, u32[]{:S(2)}) %all-to-all-start.1) | async-done | bytes 655392 | tf_op jit(solution)/shard_map/all_to_all | solution.py:47
  44.0 0.8 %gather_fusion.2 = bf16[128,256]{1,0:T(8,128)(2,1)S(1)} fusion(bf16[1280,256]{1,0:T(8,128)(2,1)S(1)} %bitcast.72, s32[1024]{0:T(1024)S(1)} %pad_clamp_fusion.1), kind=kCustom, calls=%fused_computation.2 | custom fusion | bytes 131584 | tf_op jit(solution)/shard_map/jit(_take)/gather | solution.py:49
  44.9 0.0 copy-done.5
  44.9 0.0 copy-done.6
  44.9 0.9 %convolution_convert_fusion.1 = bf16[128,512]{1,0:T(8,128)(2,1)} fusion(bf16[256,256]{1,0:T(8,128)(2,1)S(1)} %copy-done.5, bf16[256,256]{1,0:T(8,128)(2,1)S(1)} %copy-done.6, bf16[128,256]{1,0:T(8,128)(2,1)S(1)} %gather_fusion.2, pred[128]{0:T(512)(128)(4,1)S(1)} %compare_and_fusion.1), kind=kOutput, calls=%fused_computation.10 | convolution fusion | flops 34177024 | bytes 458880 | tf_op jit(solution)/shard_map/dot_general | solution.py:59
  45.8 0.0 all-gather.2.cloned.1.call-update
  46.5 0.0 copy-done.4
  46.6 0.0 copy-done.2
  46.6 1.2 %gather_fusion.1 = bf16[256,256]{1,0:T(8,128)(2,1)S(1)} fusion(bf16[1280,256]{1,0:T(8,128)(2,1)S(1)} %bitcast.73, s32[1024]{0:T(1024)S(1)} %pad_clamp_fusion.2), kind=kCustom, calls=%fused_computation.1 | custom fusion | bytes 263168 | tf_op jit(solution)/shard_map/jit(_take)/gather | solution.py:50
  47.7 0.0 copy-done
  47.7 0.3 convolution_convert_fusion
  48.0 0.0 copy-done.1
  48.1 0.3 fusion.12
  48.4 19.9 %all-gather.2.cloned.1.call-done = bf16[1024,512]{1,0:T(8,128)(2,1)} async-done(((bf16[128,512]{1,0:T(8,128)(2,1)}), bf16[1024,512]{1,0:T(8,128)(2,1)}) %all-gather.2.cloned.1.call-update) | async-done | bytes 1048592 | tf_op jit(solution)/shard_map/all_gather | solution.py:60
  68.3 1.3 %fusion.36 = (bf16[1024,256]{1,0:T(8,128)(2,1)S(1)}, bf16[1024,256]{1,0:T(8,128)(2,1)S(1)}) fusion(bf16[1024,512]{1,0:T(8,128)(2,1)} %all-gather.2.cloned.1.call-done), kind=kLoop, calls=%fused_computation.64 | loop fusion | bytes 2097152 | tf_op jit(solution)/shard_map/slice | solution.py:62
  69.6 0.2 copy.22
  69.8 0.2 copy.21
  70.0 1.6 %fusion.5 = bf16[4,64,256]{2,1,0:T(8,128)(2,1)S(1)} fusion(bf16[1024,4,64]{0,2,1:T(8,128)(2,1)S(1)} %bitcast.76, bf16[1024,4,64]{0,2,1:T(8,128)(2,1)S(1)} %bitcast.75, bf16[256,4,64]{0,2,1:T(8,128)(2,1)S(1)} %bitcast.77, pred[1024]{0:T(1024)(128)(4,1)S(1)} %iota_compare_fusion.1, f32[]{:T(128)S(6)} %sqrt.3), kind=kOutput, calls=%fused_computation.12 | convolution fusion | flops 274857984 | bytes 1311748 | tf_op jit(solution)/shard_map/bgo,ogl->bgl/dot_general | solution.py:74
  71.6 2.3 %fusion.8 = f32[1,256]{1,0:T(1,128)} fusion(bf16[1024,1]{0,1:T(2,128)(2,1)S(1)} %reshape.195, f32[256,1024]{1,0:T(8,128)S(1)} %fusion.12, bf16[256,256]{0,1:T(8,128)(2,1)S(1)} %bitcast.89, bf16[512,1024]{1,0:T(8,128)(2,1)} %param.20), kind=kOutput, calls=%fused_computation.14 | convolution fusion | flops 136314880 | bytes 1707008 | tf_op jit(solution)/shard_map/dot_general | solution.py:86
  (11 shorter events, 0.1 us)
Async XLA Ops:
  6.5 41.2 %copy-start = (bf16[256,256]{1,0:T(8,128)(2,1)S(1)}, bf16[256,256]{1,0:T(8,128)(2,1)}, u32[]{:S(2)}) copy-start(bf16[256,256]{1,0:T(8,128)(2,1)} %param.17) | copy-start | bytes 393220
  25.2 10.7 %copy-start.3 = (s32[1,128,1]{1,2,0:T(1,128)S(1)}, s32[1,128,1]{1,2,0:T(1,128)}, u32[]{:S(2)}) copy-start(s32[1,128,1]{1,2,0:T(1,128)} %param.12) | copy-start | bytes 1540
  25.2 19.7 %copy-start.5 = (bf16[256,256]{1,0:T(8,128)(2,1)S(1)}, bf16[256,256]{1,0:T(8,128)(2,1)}, u32[]{:S(2)}) copy-start(bf16[256,256]{1,0:T(8,128)(2,1)} %param.19) | copy-start | bytes 393220
  25.2 19.7 %copy-start.6 = (bf16[256,256]{1,0:T(8,128)(2,1)S(1)}, bf16[256,256]{1,0:T(8,128)(2,1)}, u32[]{:S(2)}) copy-start(bf16[256,256]{1,0:T(8,128)(2,1)} %param.18) | copy-start | bytes 393220
  25.2 21.3 %copy-start.4 = (bf16[1024]{0:T(1024)(128)(2,1)S(1)}, bf16[1024]{0:T(1024)(128)(2,1)}, u32[]{:S(2)}) copy-start(bf16[1024]{0:T(1024)(128)(2,1)} %param.21) | copy-start | bytes 6148
  25.2 21.3 %copy-start.2 = (s32[1,256,1]{1,2,0:T(1,128)S(1)}, s32[1,256,1]{1,2,0:T(1,128)}, u32[]{:S(2)}) copy-start(s32[1,256,1]{1,2,0:T(1,128)} %param.14) | copy-start | bytes 3076
  31.2 16.8 %copy-start.1 = (bf16[512,1024]{1,0:T(8,128)(2,1)S(1)}, bf16[512,1024]{1,0:T(8,128)(2,1)}, u32[]{:S(2)}) copy-start(bf16[512,1024]{1,0:T(8,128)(2,1)} %param.20) | copy-start | bytes 3145732
  32.3 11.7 %all-to-all-start.1 = ((bf16[4,320,256]{2,1,0:T(8,128)(2,1)}), bf16[4,320,256]{2,1,0:T(8,128)(2,1)S(1)}, u32[]{:S(2)}, u32[]{:S(2)}) async-start(bf16[4,320,256]{2,1,0:T(8,128)(2,1)} %broadcast_select_fusion), calls=%async_computation.1 | async-start | bytes 1310720 | tf_op jit(solution)/shard_map/all_to_all | solution.py:47
  35.8 32.5 %all-gather.2.cloned.1.call-start = ((), (), s32[]{:S(2)}) async-start(), calls=%async_computation.2 | async-start | bytes 1179648 | tf_op jit(solution)/shard_map/all_gather | solution.py:60
Sparse Core Ops, SparseCore 0:
  45.9 22.3 all-gather.1
where the time goes:
time: 81.1 us; the launch traced here: 80.8 us
  waiting for transfers between devices  28.1 us (35%)
  between operations  14.3 us (18%)
  local copies, waits for them, and re-layouts  12.8 us (16%)
  blocking collectives  9.64 us (12%)
  other arithmetic  6.98 us (9%)
  matrix products  5.39 us (7%)
  starting transfers between devices  3.52 us (4%)
    all_gather x1, waiting for transfers between devices, body(): pair_rows = lax.all_gather(pair_local, 'cand', axis=0, tiled=True)  19.9 us
    all_to_all x1, blocking collectives, body(): lax.all_to_all(wanted, 'req', split_axis=0, concat_axis=0, tiled=True)  9.64 us
    all_to_all x1, waiting for transfers between devices, body(): lax.all_to_all(fetched, 'req', split_axis=0, concat_axis=0, tiled=True)  8.15 us
    gather x1, local copies, waits for them, and re-layouts, body(): jnp.take(table, lax.all_to_all(wanted, 'req', split_axis=0, concat_axis=0...  5.95 us
    all_to_all x1, starting transfers between devices, body(): lax.all_to_all(fetched, 'req', split_axis=0, concat_axis=0, tiled=True)  3.48 us
    scatter x2, local copies, waits for them, and re-layouts, body(): wanted.at[hist_slot].set(history_row[0]).at[cand_slot].set(candidate_row[0])  2.7 us
    dot_general x1, matrix products, body(): jnp.dot(hidden, tower_out, preferred_element_type=jnp.float32)[None, :]  2.27 us
  transfers between devices with their start and end apart: 2, of which 2 were waited for; matrix products, arithmetic and copies ran while one was open for 2% of the time, Pallas kernels for 0%

commit v1 on v0

--- a/solution.py
+++ b/solution.py
@@ -5,6 +5,17 @@
 from jax.sharding import PartitionSpec as P
 
 HEADS = 4
+
+
+def in_blocks(array, dim, length):
+    before, after = (array.shape[:dim], array.shape[dim + 1 :])
+    return jnp.moveaxis(array.reshape(*before, length, -1, *after), dim, 0)
+
+
+def joined_along(tiles, dim):
+    lengths = list(tiles.shape[1:])
+    lengths[dim] *= tiles.shape[0]
+    return jnp.moveaxis(tiles, 0, dim).reshape(lengths)
 
 
 def slot_index(shard_ids, n_dest, slot_count, first_slot):
@@ -44,7 +55,14 @@
     fetched = jnp.take(
         table, lax.all_to_all(wanted, "req", split_axis=0, concat_axis=0, tiled=True), axis=0
     )
-    replies = lax.all_to_all(fetched, "req", split_axis=0, concat_axis=0, tiled=True)
+    size, here = (lax.axis_size("req"), lax.axis_index("req"))
+    parts = in_blocks(fetched, 0, size)
+    gathered = [parts[here]]
+    for turn in range(1, size):
+        sent = parts[here ^ turn]
+        gathered.append(lax.ppermute(sent, "req", [(i, i ^ turn) for i in range(size)]))
+    parts = jnp.stack(gathered)[here ^ jnp.arange(size)]
+    replies = joined_along(parts, 0)
     flat_rows = replies.reshape(n_dest * slot_count, d_model)
     hist_emb = jnp.take(flat_rows, hist_slot, axis=0)
     cand_emb = jnp.take(flat_rows, cand_slot, axis=0)

time: 81.1 us -> 78.4 us (0.967)
  blocking collectives: 9.64 us -> 0 us
  starting transfers between devices: 3.52 us -> 8.72 us
  local copies, waits for them, and re-layouts: 12.8 us -> 14 us
    all_to_all x1 -> x0, blocking collectives: 9.64 us -> none  [body(): lax.all_to_all(wanted, 'req', split_axis=0, concat_axis=0, tiled=True)]
    ppermute x0 -> x3, waiting for transfers between devices: none -> 4.8 us  [body(): lax.ppermute(sent, 'req', [(i, i ^ turn) for i in range(size)])]
    all_to_all x1, waiting for transfers between devices: 8.15 us -> 3.99 us  [body(): lax.all_to_all(wanted, 'req', split_axis=0, concat_axis=0, tiled=True)]
    ppermute x0 -> x3, starting transfers between devices: none -> 3.55 us  [body(): lax.ppermute(sent, 'req', [(i, i ^ turn) for i in range(size)])]
    all_to_all x1, starting transfers between devices: 3.48 us -> 5.16 us  [body(): lax.all_to_all(wanted, 'req', split_axis=0, concat_axis=0, tiled=True)]
    select_n x2, other arithmetic: 1.1 us -> 0.27 us  [body(): jnp.take(table, lax.all_to_all(wanted, 'req', split_axis=0, concat_axis=0...]
  transfers between devices with their start and end apart: 2 -> 5, of which waited for: 2 -> 4; matrix products, arithmetic and copies ran while one was open for 2% -> 3% of each run, Pallas kernels for 0% -> 0%
where the time goes in v1:
time: 78.4 us; the launch traced here: 78 us
  waiting for transfers between devices  28.7 us (37%)
  between operations  14.3 us (18%)
  local copies, waits for them, and re-layouts  14 us (18%)
  starting transfers between devices  8.72 us (11%)
  other arithmetic  6.9 us (9%)
  matrix products  5.39 us (7%)
    all_gather x1, waiting for transfers between devices, body(): pair_rows = lax.all_gather(pair_local, 'cand', axis=0, tiled=True)  19.9 us
    gather x1, local copies, waits for them, and re-layouts, body(): jnp.take(table, lax.all_to_all(wanted, 'req', split_axis=0, concat_axis=0...  5.86 us
    all_to_all x1, starting transfers between devices, body(): lax.all_to_all(wanted, 'req', split_axis=0, concat_axis=0, tiled=True)  5.16 us
    ppermute x3, waiting for transfers between devices, body(): lax.ppermute(sent, 'req', [(i, i ^ turn) for i in range(size)])  4.8 us
    all_to_all x1, waiting for transfers between devices, body(): lax.all_to_all(wanted, 'req', split_axis=0, concat_axis=0, tiled=True)  3.99 us
    ppermute x3, starting transfers between devices, body(): lax.ppermute(sent, 'req', [(i, i ^ turn) for i in range(size)])  3.55 us
    scatter x2, local copies, waits for them, and re-layouts, body(): wanted.at[hist_slot].set(history_row[0]).at[cand_slot].set(candidate_row[0])  2.7 us
    dot_general x1, matrix products, body(): jnp.dot(hidden, tower_out, preferred_element_type=jnp.float32)[None, :]  2.27 us
  transfers between devices with their start and end apart: 5, of which 4 were waited for; matrix products, arithmetic and copies ran while one was open for 3% of the time, Pallas kernels for 0%

profile of v1, /device:TPU:0, one launch (start us, length us, event | category | flops | bytes accessed | tf_op | source)
XLA Modules:
  0.0 78.0 jit_solution(2912909123871484966)
XLA Ops:
  6.5 0.7 compare_convert_fusion
  7.3 1.2 %reduce-window.6 = s32[4,2,128]{2,1,0:T(2,128)S(1)} reduce-window(s32[4,2,128]{2,1,0:T(2,128)S(1)} %compare_convert_fusion, s32[]{:T(128)} %constant.37.clone.1), window={size=1x1x128 pad=0_0x0_0x127_0}, to_apply=%region_0.0 | reduce-window | flops 130048 | bytes 8196 | tf_op jit(solution)/shard_map/reduce-window
  8.5 0.1 slice.32
  8.5 0.1 copy.19
  8.7 0.1 copy.20
  8.8 0.1 add_bitcast_fusion
  8.9 0.7 fusion.24
  9.6 0.7 compare_select_fusion.2
  10.2 0.7 fusion.18
  11.0 0.2 reduce_window_sum.28
  11.2 0.8 %select_reduce_fusion = s32[128]{0:T(128)S(1)} fusion(s32[128,4]{1,0:T(8,128)S(1)} %reduce_window_sum.28, s32[128]{0:T(128)} %bitcast.98), kind=kLoop, calls=%fused_computation.28 | loop fusion | flops 2432 | bytes 3072 | tf_op jit(solution)/shard_map/reduce_sum | solution.py:24
  12.0 0.7 fusion.27
  12.7 1.1 %scatter_custom_fusion = s32[1280]{0:T(1024)S(1)} fusion(s32[128]{0:T(128)S(1)} %fusion.27, s32[128]{0:T(128)} %bitcast.100, s32[]{:T(128)} %constant.37.clone.1), kind=kCustom, calls=%fused_computation.48 | custom fusion | bytes 5632 | tf_op jit(solution)/shard_map/scatter | solution.py:53
  13.8 1.6 %scatter_fusion = s32[1280]{0:T(1024)S(1)} fusion(s32[1280]{0:T(1024)S(1)} %scatter_custom_fusion, s32[256]{0:T(256)S(1)} %bitcast.93, s32[256]{0:T(256)} %bitcast.99), kind=kCustom, calls=%fused_computation.5 | custom fusion | bytes 4096 | tf_op jit(solution)/shard_map/scatter | solution.py:53
  15.4 0.7 all_to_all.10
  16.0 5.2 %all-to-all-start = ((s32[4,1,320]{2,1,0:T(1,128)}), s32[4,1,320]{2,1,0:T(1,128)S(1)}, u32[]{:S(2)}, u32[]{:S(2)}) async-start(s32[4,1,320]{2,1,0:T(1,128)} %all_to_all.10), calls=%async_computation | async-start | bytes 12288 | tf_op jit(solution)/shard_map/all_to_all | solution.py:56
  21.2 0.7 compare_and_fusion.1
  21.9 4.0 %all-to-all-done = s32[4,1,320]{2,1,0:T(1,128)S(1)} async-done(((s32[4,1,320]{2,1,0:T(1,128)}), s32[4,1,320]{2,1,0:T(1,128)S(1)}, u32[]{:S(2)}, u32[]{:S(2)}) %all-to-all-start) | async-done | bytes 5152 | tf_op jit(solution)/shard_map/all_to_all | solution.py:56
  25.9 0.1 reshape.176
  26.0 5.9 %gather_fusion = bf16[1280,256]{1,0:T(8,128)(2,1)S(1)} fusion(bf16[8192,256]{1,0:T(8,128)(2,1)} %param.11, s32[2048]{0:T(1024)S(1)} %pad_clamp_fusion), kind=kCustom, calls=%fused_computation | custom fusion | bytes 1315840 | tf_op jit(solution)/shard_map/jit(_take)/gather | solution.py:55
  31.9 0.0 copy-start.4
  31.9 0.0 copy-start.5
  31.9 0.0 copy-start.3
  31.9 0.0 copy-start.2
  31.9 0.0 copy-start.1
  32.0 0.2 broadcast_select_fusion
  32.2 0.1 dynamic-slice_bitcast_fusion
  32.3 0.6 collective-permute-start.2
  32.9 1.5 %collective-permute-start.1 = (bf16[1,320,256]{2,1,0:T(8,128)(2,1)S(1)}, bf16[1,320,256]{2,1,0:T(8,128)(2,1)S(1)}, u32[]{:S(2)}, u32[]{:S(2)}) collective-permute-start(bf16[1,320,256]{2,1,0:T(8,128)(2,1)S(1)} %get-tuple-element.9), channel_id=1, source_target_pairs={{0,16},{8,24},{16,0},{24,8},{1,17},{9,25},{17,1},{25,9},{2,18},{10... | collective-permute-start | bytes 491528 | tf_op jit(solution)/shard_map/ppermute | solution.py:63
  34.4 1.4 %collective-permute-start = (bf16[1,320,256]{2,1,0:T(8,128)(2,1)S(1)}, bf16[1,320,256]{2,1,0:T(8,128)(2,1)S(1)}, u32[]{:S(2)}, u32[]{:S(2)}) collective-permute-start(bf16[1,320,256]{2,1,0:T(8,128)(2,1)S(1)} %get-tuple-element.10), channel_id=1, source_target_pairs={{0,8},{8,0},{16,24},{24,16},{1,9},{9,1},{17,25},{25,17},{2,10},{10... | collective-permute-start | bytes 491528 | tf_op jit(solution)/shard_map/ppermute | solution.py:63
  35.8 3.8 %collective-permute-done.2 = bf16[1,320,256]{2,1,0:T(8,128)(2,1)S(1)} collective-permute-done((bf16[1,320,256]{2,1,0:T(8,128)(2,1)S(1)}, bf16[1,320,256]{2,1,0:T(8,128)(2,1)S(1)}, u32[]{:S(2)}, u32[]{:S(2)}) %collective-permute-start.2) | collective-permute-done | bytes 163872 | tf_op jit(solution)/shard_map/ppermute | solution.py:63
  39.7 1.0 %collective-permute-done.1 = bf16[1,320,256]{2,1,0:T(8,128)(2,1)S(1)} collective-permute-done((bf16[1,320,256]{2,1,0:T(8,128)(2,1)S(1)}, bf16[1,320,256]{2,1,0:T(8,128)(2,1)S(1)}, u32[]{:S(2)}, u32[]{:S(2)}) %collective-permute-start.1) | collective-permute-done | bytes 163872 | tf_op jit(solution)/shard_map/ppermute | solution.py:63
  40.6 0.0 collective-permute-done
  40.6 0.1 maximum_bitcast_fusion
  40.7 0.6 gather_fusion.1
  41.3 0.8 %gather_fusion.3 = bf16[128,256]{1,0:T(8,128)(2,1)S(1)} fusion(bf16[1280,256]{1,0:T(8,128)(2,1)S(1)} %bitcast.81, s32[1024]{0:T(1024)S(1)} %pad_clamp_fusion.1), kind=kCustom, calls=%fused_computation.3 | custom fusion | bytes 131584 | tf_op jit(solution)/shard_map/jit(_take)/gather | solution.py:67
  42.2 0.0 copy-done.4
  42.2 0.9 %convolution_convert_fusion.1 = bf16[128,512]{1,0:T(8,128)(2,1)} fusion(bf16[256,256]{1,0:T(8,128)(2,1)S(1)} %copy-done.4, bf16[256,256]{1,0:T(8,128)(2,1)S(1)} %copy-done.5, bf16[128,256]{1,0:T(8,128)(2,1)S(1)} %gather_fusion.3, pred[128]{0:T(512)(128)(4,1)S(1)} %compare_and_fusion.1), kind=kOutput, calls=%fused_computation.11 | convolution fusion | flops 34177024 | bytes 458880 | tf_op jit(solution)/shard_map/dot_general | solution.py:77
  43.1 0.0 all-gather.2.cloned.1.call-update
  43.9 1.2 %gather_fusion.2 = bf16[256,256]{1,0:T(8,128)(2,1)S(1)} fusion(bf16[1280,256]{1,0:T(8,128)(2,1)S(1)} %bitcast.82, s32[1024]{0:T(1024)S(1)} %pad_clamp_fusion.2), kind=kCustom, calls=%fused_computation.2 | custom fusion | bytes 263168 | tf_op jit(solution)/shard_map/jit(_take)/gather | solution.py:68
  45.0 0.3 convolution_convert_fusion
  45.3 0.3 fusion.12
  45.7 19.9 %all-gather.2.cloned.1.call-done = bf16[1024,512]{1,0:T(8,128)(2,1)} async-done(((bf16[128,512]{1,0:T(8,128)(2,1)}), bf16[1024,512]{1,0:T(8,128)(2,1)}) %all-gather.2.cloned.1.call-update) | async-done | bytes 1048592 | tf_op jit(solution)/shard_map/all_gather | solution.py:78
  65.6 1.3 %fusion.37 = (bf16[1024,256]{1,0:T(8,128)(2,1)S(1)}, bf16[1024,256]{1,0:T(8,128)(2,1)S(1)}) fusion(bf16[1024,512]{1,0:T(8,128)(2,1)} %all-gather.2.cloned.1.call-done), kind=kLoop, calls=%fused_computation.73 | loop fusion | bytes 2097152 | tf_op jit(solution)/shard_map/slice | solution.py:80
  66.9 0.2 copy.22
  67.1 0.2 copy.21
  67.3 1.6 %fusion.5 = bf16[4,64,256]{2,1,0:T(8,128)(2,1)S(1)} fusion(bf16[1024,4,64]{0,2,1:T(8,128)(2,1)S(1)} %bitcast.85, bf16[1024,4,64]{0,2,1:T(8,128)(2,1)S(1)} %bitcast.84, bf16[256,4,64]{0,2,1:T(8,128)(2,1)S(1)} %bitcast.89, pred[1024]{0:T(1024)(128)(4,1)S(1)} %iota_compare_fusion.1, f32[]{:T(128)S(6)} %sqrt.3), kind=kOutput, calls=%fused_computation.13 | convolution fusion | flops 274857984 | bytes 1311748 | tf_op jit(solution)/shard_map/bgo,ogl->bgl/dot_general | solution.py:92
  68.9 2.3 %fusion.8 = f32[1,256]{1,0:T(1,128)} fusion(bf16[1024,1]{0,1:T(2,128)(2,1)S(1)} %reshape.226, f32[256,1024]{1,0:T(8,128)S(1)} %fusion.12, bf16[256,256]{0,1:T(8,128)(2,1)S(1)} %bitcast.101, bf16[512,1024]{1,0:T(8,128)(2,1)} %param.20), kind=kOutput, calls=%fused_computation.15 | convolution fusion | flops 136314880 | bytes 1707008 | tf_op jit(solution)/shard_map/dot_general | solution.py:104
  (19 shorter events, 0.2 us)
Async XLA Ops:
  6.5 38.5 %copy-start = (bf16[256,256]{1,0:T(8,128)(2,1)S(1)}, bf16[256,256]{1,0:T(8,128)(2,1)}, u32[]{:S(2)}) copy-start(bf16[256,256]{1,0:T(8,128)(2,1)} %param.17) | copy-start | bytes 393220
  16.0 9.8 %all-to-all-start = ((s32[4,1,320]{2,1,0:T(1,128)}), s32[4,1,320]{2,1,0:T(1,128)S(1)}, u32[]{:S(2)}, u32[]{:S(2)}) async-start(s32[4,1,320]{2,1,0:T(1,128)} %all_to_all.10), calls=%async_computation | async-start | bytes 12288 | tf_op jit(solution)/shard_map/all_to_all | solution.py:56
  21.2 44.4 %all-gather.2.cloned.1.call-start = ((), (), s32[]{:S(2)}) async-start(), calls=%async_computation.1 | async-start | bytes 1179648 | tf_op jit(solution)/shard_map/all_gather | solution.py:78
  31.9 10.3 %copy-start.4 = (bf16[256,256]{1,0:T(8,128)(2,1)S(1)}, bf16[256,256]{1,0:T(8,128)(2,1)}, u32[]{:S(2)}) copy-start(bf16[256,256]{1,0:T(8,128)(2,1)} %param.19) | copy-start | bytes 393220
  31.9 10.3 %copy-start.5 = (bf16[256,256]{1,0:T(8,128)(2,1)S(1)}, bf16[256,256]{1,0:T(8,128)(2,1)}, u32[]{:S(2)}) copy-start(bf16[256,256]{1,0:T(8,128)(2,1)} %param.18) | copy-start | bytes 393220
  31.9 11.9 %copy-start.3 = (bf16[1024]{0:T(1024)(128)(2,1)S(1)}, bf16[1024]{0:T(1024)(128)(2,1)}, u32[]{:S(2)}) copy-start(bf16[1024]{0:T(1024)(128)(2,1)} %param.21) | copy-start | bytes 6148
  31.9 11.9 %copy-start.2 = (s32[1,256,1]{1,2,0:T(1,128)S(1)}, s32[1,256,1]{1,2,0:T(1,128)}, u32[]{:S(2)}) copy-start(s32[1,256,1]{1,2,0:T(1,128)} %param.14) | copy-start | bytes 3076
  31.9 13.4 %copy-start.1 = (bf16[512,1024]{1,0:T(8,128)(2,1)S(1)}, bf16[512,1024]{1,0:T(8,128)(2,1)}, u32[]{:S(2)}) copy-start(bf16[512,1024]{1,0:T(8,128)(2,1)} %param.20) | copy-start | bytes 3145732
  32.3 7.4 %collective-permute-start.2 = (bf16[1,320,256]{2,1,0:T(8,128)(2,1)S(1)}, bf16[1,320,256]{2,1,0:T(8,128)(2,1)S(1)}, u32[]{:S(2)}, u32[]{:S(2)}) collective-permute-start(bf16[1,320,256]{2,1,0:T(8,128)(2,1)S(1)} %get-tuple-element.8), channel_id=1, source_target_pairs={{0,24},{8,16},{16,8},{24,0},{1,25},{9,17},{17,9},{25,1},{2,26},{10... | collective-permute-start | bytes 491528 | tf_op jit(solution)/shard_map/ppermute | solution.py:63
  32.9 7.7 %collective-permute-start.1 = (bf16[1,320,256]{2,1,0:T(8,128)(2,1)S(1)}, bf16[1,320,256]{2,1,0:T(8,128)(2,1)S(1)}, u32[]{:S(2)}, u32[]{:S(2)}) collective-permute-start(bf16[1,320,256]{2,1,0:T(8,128)(2,1)S(1)} %get-tuple-element.9), channel_id=1, source_target_pairs={{0,16},{8,24},{16,0},{24,8},{1,17},{9,25},{17,1},{25,9},{2,18},{10... | collective-permute-start | bytes 491528 | tf_op jit(solution)/shard_map/ppermute | solution.py:63
  34.4 6.3 %collective-permute-start = (bf16[1,320,256]{2,1,0:T(8,128)(2,1)S(1)}, bf16[1,320,256]{2,1,0:T(8,128)(2,1)S(1)}, u32[]{:S(2)}, u32[]{:S(2)}) collective-permute-start(bf16[1,320,256]{2,1,0:T(8,128)(2,1)S(1)} %get-tuple-element.10), channel_id=1, source_target_pairs={{0,8},{8,0},{16,24},{24,16},{1,9},{9,1},{17,25},{25,17},{2,10},{10... | collective-permute-start | bytes 491528 | tf_op jit(solution)/shard_map/ppermute | solution.py:63
Sparse Core Ops, SparseCore 0:
  43.2 22.3 all-gather.1
